TPU v7x, 32 devices: a whole 2x2x4 slice. The times are simulated.
32 devices in a mesh: fsdp: 4 (over y, x), seq: 8 (over z, core).
Axes of the slice: x: 2, y: 2, z: 4, core: 2. Of those that a mesh axis runs over, the one named last changes fastest.
Arguments:
- events: bfloat16 [4, 1024, 2048], P('fsdp', 'seq'), may hold values from -6 to 6
- type_ids: int32 [4, 1024], P('fsdp', 'seq'), may hold values from 0 to 255
- type_table: bfloat16 [256, 2048], P('fsdp'), may hold values from -6 to 6
- norm_gain: float32 [2048], replicated, may hold values from 0.25 to 1.75
- kernel: bfloat16 [2048, 1152], P('fsdp'), may hold values from -0.1875 to 0.1875
- upstream: bfloat16 [4, 1024, 2048], P('fsdp', 'seq'), may hold values from -6 to 6
Outputs:
- input_grad: bfloat16 [4, 1024, 2048], P('fsdp', 'seq')
- table_grad: float32 [256, 2048], P(('fsdp', 'seq'))
- gain_grad: float32 [2048], P(('fsdp', 'seq'))
- kernel_grad: float32 [2048, 1152], P('seq')
All inputs are finite; a program needn't handle non-finite values.
Results may differ from a plain program's by a relative error of at most 0.0053.
Values may be sent and summed in bfloat16 or wider, within the bound.
No kernel may reach another device: no remote copies, remote signals or barrier semaphores. Data moves between devices by JAX's collectives and lax.ppermute only.
A program may use at most 128 MiB of HBM per device.

v0:
```python
import jax
import jax.numpy as jnp
from jax import lax
from jax.sharding import PartitionSpec as P

GROUPS = 16
KERNEL = 9


def with_halo(cells, sides, width):
    for axis, dim in sides:
        count = lax.axis_size(axis)
        ends = count - 1
        head = lax.slice_in_dim(cells, 0, width, axis=dim)
        tail = lax.slice_in_dim(cells, cells.shape[dim] - width, cells.shape[dim], axis=dim)
        cells = jnp.concatenate(
            [
                lax.ppermute(tail, axis, [(i, (i + 1) % count) for i in range(ends)]),
                cells,
                lax.ppermute(head, axis, [((i + 1) % count, i) for i in range(ends)]),
            ],
            axis=dim,
        )
    return cells


def from_partner(value, axis, apart):
    mask = 2**apart
    pairs = [(source, source ^ mask) for source in range(lax.axis_size(axis))]
    return lax.ppermute(value, axis, pairs)


def body(events, type_ids, type_table, norm_gain, kernel, upstream):
    length = events.shape[1]
    width = events.shape[2]
    chans = width // GROUPS
    half = KERNEL // 2
    seq_count = lax.axis_size("seq")
    total = length * seq_count * lax.axis_size("fsdp")
    scale = 1.0 / jnp.sqrt(jnp.float32(total))
    table = lax.all_gather(type_table, "fsdp", axis=0, tiled=True)
    onehot = (type_ids[0][:, None] == jnp.arange(table.shape[0], dtype=jnp.int32)[None, :]).astype(
        jnp.bfloat16
    )
    mixed = events[0].astype(jnp.float32) + jnp.dot(
        onehot, table, preferred_element_type=jnp.float32
    )
    inv = lax.rsqrt(jnp.mean(mixed * mixed, axis=-1, keepdims=True) + 1e-06)
    normed = (mixed * inv * norm_gain).astype(jnp.bfloat16)
    padded = with_halo(normed, (("seq", 0),), half)
    padded = padded.reshape(length + 2 * half, GROUPS, chans)
    weights = lax.all_gather(kernel, "fsdp", axis=0, tiled=True).reshape(
        GROUPS, chans, KERNEL, chans
    )
    conv = jnp.zeros((length, GROUPS, chans), jnp.float32)
    for k in range(KERNEL):
        conv = conv + jnp.einsum(
            "tgc,goc->tgo",
            padded[k : k + length],
            weights[:, :, k, :],
            preferred_element_type=jnp.float32,
        )
    up_float = upstream[0].astype(jnp.float32)
    sig = jax.nn.sigmoid(conv)
    dconv = (up_float.reshape(length, GROUPS, chans) * sig * (1.0 + conv * (1.0 - sig))).astype(
        jnp.bfloat16
    )
    dflat = dconv.reshape(length, width)
    dpad = with_halo(dflat, (("seq", 0),), half)
    dpad = dpad.reshape(length + 2 * half, GROUPS, chans)
    dnormed = jnp.zeros((length, GROUPS, chans), jnp.float32)
    for k in range(KERNEL):
        dnormed = dnormed + jnp.einsum(
            "tgo,goc->tgc",
            dpad[2 * half - k : 2 * half - k + length],
            weights[:, :, k, :],
            preferred_element_type=jnp.float32,
        )
    slice_width = width // seq_count
    normed_slice, dconv_slice = (
        lax.all_to_all(normed, "seq", split_axis=1, concat_axis=0, tiled=True),
        lax.all_to_all(dflat, "seq", split_axis=1, concat_axis=0, tiled=True),
    )
    whole = normed_slice.shape[0]
    if slice_width < chans:
        spread = chans // slice_width
        position = lax.axis_index("seq")
        group_rows = normed_slice
        for bit in range(spread.bit_length() - 1):
            partner = from_partner(group_rows, "seq", bit)
            lower = position >> bit & 1 == 0
            group_rows = jnp.where(
                lower,
                jnp.concatenate([group_rows, partner], axis=1),
                jnp.concatenate([partner, group_rows], axis=1),
            )
        group_in = group_rows.reshape(whole, 1, chans)
        group_out = dconv_slice.reshape(whole, 1, slice_width)
    else:
        local_groups = slice_width // chans
        group_in = normed_slice.reshape(whole, local_groups, chans)
        group_out = dconv_slice.reshape(whole, local_groups, chans)
    group_pad = jnp.pad(group_in, ((half, half), (0, 0), (0, 0)))
    kterms = []
    for k in range(KERNEL):
        kterms.append(
            jnp.einsum(
                "tgo,tgc->goc",
                group_out,
                group_pad[k : k + whole],
                preferred_element_type=jnp.float32,
            )
        )
    kernel_part = jnp.stack(kterms, axis=2).reshape(slice_width, KERNEL * chans) * scale
    kernel_grad = lax.psum(kernel_part, "fsdp")
    dnormed = dnormed.reshape(length, width)
    gain_term = jnp.sum(dnormed * mixed * inv, axis=0) * scale
    scaled = norm_gain * dnormed
    dmixed = inv * scaled - mixed * inv * inv * inv * jnp.mean(
        scaled * mixed, axis=-1, keepdims=True
    )
    input_grad = (up_float + dmixed).astype(jnp.bfloat16)
    table_term = (
        lax.dot_general(
            onehot, input_grad, (((0,), (0,)), ((), ())), preferred_element_type=jnp.float32
        )
        * scale
    )
    table_grad, gain_grad = (
        lax.psum_scatter(table_term, ("fsdp", "seq"), scatter_dimension=0, tiled=True),
        lax.psum_scatter(gain_term, ("fsdp", "seq"), scatter_dimension=0, tiled=True),
    )
    return (input_grad[None], table_grad, gain_grad, kernel_grad)


def solution(mesh):
    return jax.shard_map(
        body,
        mesh=mesh,
        in_specs=(
            P("fsdp", "seq", None),
            P("fsdp", "seq"),
            P("fsdp", None),
            P(),
            P("fsdp", None),
            P("fsdp", "seq", None),
        ),
        out_specs=(
            P("fsdp", "seq", None),
            P(("fsdp", "seq"), None),
            P(("fsdp", "seq")),
            P("seq", None),
        ),
        check_vma=False,
    )
```

profile of v0, /device:TPU:0, one launch (start us, length us, event | category | flops | bytes accessed | tf_op | source)
XLA Modules:
  0.0 384.2 jit_solution(598750002941307094)
XLA Ops:
  7.2 0.7 all-gather.3.cloned.1.call-update
  8.0 0.7 all-gather.5.cloned.1.call-update
  8.7 30.6 %all-gather.3.cloned.1.call-done = bf16[256,2048]{1,0:T(8,128)(2,1)} async-done(((bf16[64,2048]{1,0:T(8,128)(2,1)}), bf16[256,2048]{1,0:T(8,128)(2,1)}) %all-gather.3.cloned.1.call-update) | async-done | bytes 1048592 | tf_op jit(solution)/shard_map/all_gather | solution.py:41
  39.2 1.7 multiply_reduce_fusion.2
  41.1 1.0 copy.192
  42.1 4.6 %all-to-all-start.1 = ((bf16[128,8,256]{0,2,1:T(8,128)(2,1)}), bf16[128,8,256]{0,2,1:T(8,128)(2,1)S(1)}, u32[]{:S(2)}, u32[]{:S(2)}) async-start(bf16[128,8,256]{0,2,1:T(8,128)(2,1)} %bitcast.30), calls=%async_computation.2 | async-start | bytes 1048576 | tf_op jit(solution)/shard_map/all_to_all | solution.py:81
  46.7 2.4 collective-permute-start
  49.1 1.3 collective-permute-start.1
  50.6 1.2 copy.213
  51.7 1.6 collective-permute-done.1
  53.4 2.7 fusion.52
  56.0 6.0 %all-to-all-done.1 = bf16[128,8,256]{0,2,1:T(8,128)(2,1)S(1)} async-done(((bf16[128,8,256]{0,2,1:T(8,128)(2,1)}), bf16[128,8,256]{0,2,1:T(8,128)(2,1)S(1)}, u32[]{:S(2)}, u32[]{:S(2)}) %all-to-all-start.1) | async-done | bytes 524320 | tf_op jit(solution)/shard_map/all_to_all | solution.py:81
  62.6 1.0 copy.169
  63.7 34.5 %all-gather.5.cloned.1.call-done = bf16[2048,1152]{1,0:T(8,128)(2,1)} async-done(((bf16[512,1152]{1,0:T(8,128)(2,1)}), bf16[2048,1152]{1,0:T(8,128)(2,1)}) %all-gather.5.cloned.1.call-update) | async-done | bytes 4718608 | tf_op jit(solution)/shard_map/all_gather | solution.py:52
  98.2 10.5 %reshape.88 = bf16[16,128,9,128]{3,2,1,0:T(8,128)(2,1)} reshape(bf16[2048,1152]{1,0:T(8,128)(2,1)} %all-gather.5.cloned.1.call-done) | data formatting | bytes 9437184 | tf_op jit(solution)/shard_map/reshape | solution.py:52
  108.6 19.8 %fusion.82 = (bf16[16,128,1,128]{3,2,1,0:T(2,128)(2,1)S(1)}, bf16[16,128,1,128]{3,2,1,0:T(2,128)(2,1)S(1)}, bf16[16,128,1,128]{3,2,1,0:T(2,128)(2,1)S(1)}, bf16[...) fusion(bf16[16,128,9,128]{3,2,1,0:T(8,128)(2,1)} %reshape.88), kind=kLoop, calls=%fused_computation.154 | loop fusion | bytes 9437184 | tf_op jit(solution)/shard_map/slice | solution.py:60
  129.0 0.9 copy-done.22
  130.5 0.9 copy-done.21
  131.8 0.7 copy-done.20
  136.1 0.7 copy-done.25
  137.0 0.8 fusion.14
  137.9 1.1 copy.145
  138.9 1.3 collective-permute-start.2
  140.2 1.1 copy.155
  141.3 3.8 collective-permute-start.3
  145.1 2.7 fusion.63
  147.8 1.0 copy.144
  148.8 4.7 %all-to-all-start = ((bf16[128,8,256]{0,2,1:T(8,128)(2,1)}), bf16[128,8,256]{0,2,1:T(8,128)(2,1)S(1)}, u32[]{:S(2)}, u32[]{:S(2)}) async-start(bf16[128,8,256]{0,2,1:T(8,128)(2,1)} %bitcast.28), calls=%async_computation.1 | async-start | bytes 1048576 | tf_op jit(solution)/shard_map/all_to_all | solution.py:82
  153.7 6.9 %pad_maximum_fusion = (bf16[128,2048]{0,1:T(8,128)(2,1)S(1)}, bf16[128,2048]{0,1:T(8,128)(2,1)S(1)}, bf16[128,2048]{0,1:T(8,128)(2,1)S(1)}, bf16[128,2048]{0,1:T...) fusion(bf16[128,2048]{0,1:T(8,128)(2,1)} %bitcast.13, ...), kind=kLoop, calls=%fused_computation.105 | loop fusion | flops 8388608 | bytes 4751360 | tf_op jit(solution)/shard_map/concatenate | solution.py:16
  161.0 0.8 copy-done.7
  162.2 0.9 copy-done.5
  163.4 0.9 copy-done.12
  165.0 0.9 copy-done.3
  166.2 0.9 copy-done.1
  167.8 0.8 copy-done.15
  168.6 1.3 convolution_add_fusion.1
  170.0 1.6 copy.191
  171.5 1.1 copy.166
  172.7 1.3 reshape.83
  174.0 1.4 fusion.10
  178.0 1.9 copy.171
  180.0 2.4 copy.284
  182.7 0.7 copy-done.17
  183.8 1.9 convolution_multiply_fusion
  185.7 39.9 %all-reduce.1 = f32[2048]{0:T(1024)S(1)} all-reduce(f32[2048]{0:T(1024)S(1)} %broadcast_multiply_fusion.1), channel_id=3, replica_groups=mesh['fsdp'=4,'seq'=8] {'fsdp','seq'}, use_global_device_ids=true, to_apply=%region_4.5.clone | all-reduce | flops 2048 | bytes 16384
  226.2 11.7 %all-reduce.4.cloned.1.call-done = f32[256,1152]{0,1:T(8,128)} async-done(((f32[256,1152]{0,1:T(8,128)}), f32[256,1152]{0,1:T(8,128)}) %all-reduce.4.cloned.1.call-update) | async-done | bytes 1179664 | tf_op jit(solution)/shard_map/psum | solution.py:115
  237.9 2.7 copy.172
  240.6 137.1 %reduce-scatter.2.cloned.1.call-done = f32[8,2048]{1,0:T(8,128)} async-done(((f32[256,2048]{1,0:T(8,128)}), f32[8,2048]{1,0:T(8,128)}) %reduce-scatter.2.cloned.1.call-update) | async-done | bytes 65552 | tf_op jit(solution)/shard_map/reduce_scatter | solution.py:130
  (97 shorter events, 13.1 us)
Async XLA Ops:
  7.2 32.1 %copy-start.30 = (s32[1,128]{1,0:T(1,128)S(1)}, s32[1,128]{1,0:T(1,128)}, u32[]{:S(2)}) copy-start(s32[1,128]{1,0:T(1,128)} %param.7) | copy-start | bytes 1540
  7.2 32.1 %copy-start.26 = (bf16[1,128,2048]{2,1,0:T(8,128)(2,1)S(1)}, bf16[1,128,2048]{2,1,0:T(8,128)(2,1)}, u32[]{:S(2)}) copy-start(bf16[1,128,2048]{2,1,0:T(8,128)(2,1)} %param.6) | copy-start | bytes 1572868
  7.2 32.0 %all-gather.3.cloned.1.call-start = ((), (), s32[]{:S(2)}) async-start(), calls=%async_computation.3 | async-start | bytes 1310720 | tf_op jit(solution)/shard_map/all_gather | solution.py:41
  7.9 90.2 %all-gather.5.cloned.1.call-start = ((), (), s32[]{:S(2)}) async-start(), calls=%async_computation.4 | async-start | bytes 5898240 | tf_op jit(solution)/shard_map/all_gather | solution.py:52
  39.2 1.7 copy-start.29
  41.1 9.4 %copy-start.16 = (bf16[1,128,2048]{2,1,0:T(8,128)(2,1)S(1)}, bf16[1,128,2048]{2,1,0:T(8,128)(2,1)}, u32[]{:S(2)}) copy-start(bf16[1,128,2048]{2,1,0:T(8,128)(2,1)} %param.11) | copy-start | bytes 1572868
  42.1 20.0 %all-to-all-start.1 = ((bf16[128,8,256]{0,2,1:T(8,128)(2,1)}), bf16[128,8,256]{0,2,1:T(8,128)(2,1)S(1)}, u32[]{:S(2)}, u32[]{:S(2)}) async-start(bf16[128,8,256]{0,2,1:T(8,128)(2,1)} %bitcast.30), calls=%async_computation.2 | async-start | bytes 1048576 | tf_op jit(solution)/shard_map/all_to_all | solution.py:81
  46.7 5.0 %collective-permute-start = (bf16[4,2048]{1,0:T(4,128)(2,1)S(1)}, bf16[4,2048]{1,0:T(4,128)(2,1)S(1)}, u32[]{:S(2)}, u32[]{:S(2)}) collective-permute-start(bf16[4,2048]{1,0:T(4,128)(2,1)S(1)} %get-tuple-element.54), channel_id=1, source_target_pairs={{0,1},{1,2},{2,3},{3,4},{4,5},{5,6},{6,7},{8,9},{9,10},{10,11},{11... | collective-permute-start | bytes 49160 | tf_op jit(solution)/shard_map/ppermute | solution.py:18
  49.1 4.2 %collective-permute-start.1 = (bf16[4,2048]{1,0:T(4,128)(2,1)S(1)}, bf16[4,2048]{1,0:T(4,128)(2,1)S(1)}, u32[]{:S(2)}, u32[]{:S(2)}) collective-permute-start(bf16[4,2048]{1,0:T(4,128)(2,1)S(1)} %get-tuple-element.53), channel_id=1, source_target_pairs={{1,0},{2,1},{3,2},{4,3},{5,4},{6,5},{7,6},{9,8},{10,9},{11,10},{12... | collective-permute-start | bytes 49160 | tf_op jit(solution)/shard_map/ppermute | solution.py:20
  108.6 19.9 %copy-start.23 = (bf16[16,16,8,128]{3,2,1,0:T(8,128)(2,1)S(1)}, bf16[16,16,8,128]{3,2,1,0:T(8,128)(2,1)}, u32[]{:S(2)}) copy-start(bf16[16,16,8,128]{3,2,1,0:T(8,128)(2,1)} %get-tuple-element.51) | copy-start | bytes 1572868
  128.4 2.0 copy-start.6
  128.4 2.0 copy-start.8
  128.5 2.0 copy-start.4
  128.5 3.4 copy-start.11
  128.5 4.6 %copy-start.10 = (bf16[16,128,1,128]{3,2,1,0:T(2,128)(2,1)}, bf16[16,128,1,128]{3,2,1,0:T(2,128)(2,1)S(1)}, u32[]{:S(2)}) copy-start(bf16[16,128,1,128]{3,2,1,0:T(2,128)(2,1)S(1)} %get-tuple-element.22) | copy-start | bytes 1572868
  128.5 5.1 %copy-start.2 = (bf16[16,128,1,128]{3,2,1,0:T(2,128)(2,1)}, bf16[16,128,1,128]{3,2,1,0:T(2,128)(2,1)S(1)}, u32[]{:S(2)}) copy-start(bf16[16,128,1,128]{3,2,1,0:T(2,128)(2,1)S(1)} %get-tuple-element.21) | copy-start | bytes 1572868
  128.5 6.1 %copy-start = (bf16[16,128,1,128]{3,2,1,0:T(2,128)(2,1)}, bf16[16,128,1,128]{3,2,1,0:T(2,128)(2,1)S(1)}, u32[]{:S(2)}) copy-start(bf16[16,128,1,128]{3,2,1,0:T(2,128)(2,1)S(1)} %get-tuple-element.20) | copy-start | bytes 1572868
  128.5 7.6 %copy-start.14 = (bf16[16,128,1,128]{3,2,1,0:T(2,128)(2,1)}, bf16[16,128,1,128]{3,2,1,0:T(2,128)(2,1)S(1)}, u32[]{:S(2)}) copy-start(bf16[16,128,1,128]{3,2,1,0:T(2,128)(2,1)S(1)} %get-tuple-element.18) | copy-start | bytes 1572868
  128.5 1.4 copy-start.22
  129.9 1.4 copy-start.21
  131.3 1.2 copy-start.20
  133.0 1.0 copy-start.19
  134.1 1.0 copy-start.18
  135.6 1.2 copy-start.25
  135.6 1.3 copy-start.27
  138.9 14.8 %collective-permute-start.2 = (bf16[4,2048]{0,1:T(8,128)(2,1)}, bf16[4,2048]{0,1:T(8,128)(2,1)}, u32[]{:S(2)}, u32[]{:S(2)}) collective-permute-start(bf16[4,2048]{0,1:T(8,128)(2,1)} %copy.145), channel_id=1, source_target_pairs={{1,0},{2,1},{3,2},{4,3},{5,4},{6,5},{7,6},{9,8},{10,9},{11,10},{12... | collective-permute-start | bytes 49160 | tf_op jit(solution)/shard_map/ppermute | solution.py:20
  141.3 12.4 %collective-permute-start.3 = (bf16[4,2048]{0,1:T(8,128)(2,1)}, bf16[4,2048]{0,1:T(8,128)(2,1)}, u32[]{:S(2)}, u32[]{:S(2)}) collective-permute-start(bf16[4,2048]{0,1:T(8,128)(2,1)} %copy.155), channel_id=1, source_target_pairs={{0,1},{1,2},{2,3},{3,4},{4,5},{5,6},{6,7},{8,9},{9,10},{10,11},{11... | collective-permute-start | bytes 49160 | tf_op jit(solution)/shard_map/ppermute | solution.py:18
  148.8 22.7 %all-to-all-start = ((bf16[128,8,256]{0,2,1:T(8,128)(2,1)}), bf16[128,8,256]{0,2,1:T(8,128)(2,1)S(1)}, u32[]{:S(2)}, u32[]{:S(2)}) async-start(bf16[128,8,256]{0,2,1:T(8,128)(2,1)} %bitcast.28), calls=%async_computation.1 | async-start | bytes 1048576 | tf_op jit(solution)/shard_map/all_to_all | solution.py:82
  153.5 84.4 %all-reduce.4.cloned.1.call-start = ((), (), s32[]{:S(2)}) async-start(), calls=%async_computation.6 | async-start | bytes 2359296 | tf_op jit(solution)/shard_map/psum | solution.py:115
  153.7 6.9 %copy-start.9 = (bf16[16,128,1,128]{3,2,1,0:T(2,128)(2,1)S(1)}, bf16[16,128,1,128]{3,2,1,0:T(2,128)(2,1)}, u32[]{:S(2)}) copy-start(bf16[16,128,1,128]{3,2,1,0:T(2,128)(2,1)} %copy-done.8) | copy-start | bytes 1572868
  160.6 1.2 copy-start.7
  161.8 1.2 copy-start.5
  163.1 1.2 copy-start.12
  163.1 1.5 copy-start.13
  164.6 1.2 copy-start.3
  165.8 1.2 copy-start.1
  167.4 1.2 copy-start.15
  173.9 1.4 copy-start.28
  182.3 1.0 copy-start.17
  182.4 195.3 %reduce-scatter.2.cloned.1.call-start = ((), (), s32[]{:S(2)}) async-start(), calls=%async_computation.5 | async-start | bytes 2162688 | tf_op jit(solution)/shard_map/reduce_scatter | solution.py:130
  183.8 1.9 copy-start.24
Sparse Core Ops, SparseCore 0:
  9.9 29.3 all-gather.2
  41.1 57.0 all-gather.4
  182.5 55.3 all-reduce.3
  240.7 136.9 reduce-scatter.1
where the time goes:
time: 386 us; the launch traced here: 384 us
  waiting for transfers between devices  223 us (58%)
  local copies, waits for them, and re-layouts  59.2 us (15%)
  blocking collectives  39.9 us (10%)
  matrix products  18.8 us (5%)
  starting transfers between devices  18.4 us (5%)
  between operations  14.4 us (4%)
  other arithmetic  10.6 us (3%)
    reduce_scatter x1, waiting for transfers between devices, body(): lax.psum_scatter(table_term, ('fsdp', 'seq'), scatter_dimension=0, tiled=...  137 us
    unnamed x1, blocking collectives  39.9 us
    all_gather x1, waiting for transfers between devices, body(): lax.all_gather(kernel, 'fsdp', axis=0, tiled=True)  34.5 us
    all_gather x1, waiting for transfers between devices, body(): table = lax.all_gather(type_table, 'fsdp', axis=0, tiled=True)  30.6 us
    slice x1, local copies, waits for them, and re-layouts, body(): weights[:, :, k, :]  19.8 us
    unnamed x66, local copies, waits for them, and re-layouts  17.4 us
    psum x1, waiting for transfers between devices, body(): kernel_grad = lax.psum(kernel_part, 'fsdp')  11.7 us
    reshape x1, local copies, waits for them, and re-layouts, body(): lax.all_gather(kernel, 'fsdp', axis=0, tiled=True)  10.5 us
  transfers between devices with their start and end apart: 10, of which 6 were waited for; matrix products, arithmetic and copies ran while one was open for 8% of the time, Pallas kernels for 0%

commit v1 on v0

--- a/solution.py
+++ b/solution.py
@@ -1,3 +1,4 @@
+import functools
 import jax
 import jax.numpy as jnp
 from jax import lax
@@ -5,6 +6,22 @@
 
 GROUPS = 16
 KERNEL = 9
+
+
+def draft_classes_here(u_in, at_axis):
+    degree = lax.axis_size("fsdp")
+    mat_out = u_in
+    block_next = [(nth - 1, nth) for nth in range(1, degree)] + [(degree - 1, 0)]
+    rows = [mat_out]
+    for _ in tuple(range(degree - 1)):
+        mat_out = lax.ppermute(mat_out, axis_name="fsdp", perm=block_next)
+        rows += [mat_out]
+    ready = jnp.concatenate([*reversed(rows)], at_axis)
+    oldest = lax.axis_index("fsdp")
+    return jnp.roll(ready, (oldest + 1) * mat_out.shape[at_axis], at_axis)
+
+
+weights_edit = functools.partial(draft_classes_here, at_axis=0)
 
 
 def with_halo(cells, sides, width):
@@ -38,7 +55,7 @@
     seq_count = lax.axis_size("seq")
     total = length * seq_count * lax.axis_size("fsdp")
     scale = 1.0 / jnp.sqrt(jnp.float32(total))
-    table = lax.all_gather(type_table, "fsdp", axis=0, tiled=True)
+    table = weights_edit(type_table)
     onehot = (type_ids[0][:, None] == jnp.arange(table.shape[0], dtype=jnp.int32)[None, :]).astype(
         jnp.bfloat16
     )

time: 386 us -> 365 us (0.946)
  waiting for transfers between devices: 223 us -> 197 us
  starting transfers between devices: 18.4 us -> 23.3 us
    ppermute x0 -> x3, waiting for transfers between devices: none -> 32.1 us  [draft_classes_here(): mat_out = lax.ppermute(mat_out, axis_name='fsdp', perm=block_next)]
    all_gather x1 -> x0, waiting for transfers between devices: 30.6 us -> none  [body(): table = lax.all_gather(type_table, 'fsdp', axis=0, tiled=True)]
    all_gather x1, waiting for transfers between devices: 34.5 us -> 7.95 us  [body(): lax.all_gather(kernel, 'fsdp', axis=0, tiled=True)]
    ppermute x0 -> x3, starting transfers between devices: none -> 4.77 us  [draft_classes_here(): mat_out = lax.ppermute(mat_out, axis_name='fsdp', perm=block_next)]
    unnamed x66 -> x75, local copies, waits for them, and re-layouts: 17.4 us -> 18.9 us
  transfers between devices with their start and end apart: 10 -> 12, of which waited for: 6 -> 8; matrix products, arithmetic and copies ran while one was open for 8% -> 8% of each run, Pallas kernels for 0% -> 0%
where the time goes in v1:
time: 365 us; the launch traced here: 363 us
  waiting for transfers between devices  197 us (54%)
  local copies, waits for them, and re-layouts  60.1 us (16%)
  blocking collectives  39.9 us (11%)
  starting transfers between devices  23.3 us (6%)
  matrix products  17.5 us (5%)
  between operations  14.4 us (4%)
  other arithmetic  10.6 us (3%)
    reduce_scatter x1, waiting for transfers between devices, body(): lax.psum_scatter(table_term, ('fsdp', 'seq'), scatter_dimension=0, tiled=...  137 us
    unnamed x1, blocking collectives  39.9 us
    ppermute x3, waiting for transfers between devices, draft_classes_here(): mat_out = lax.ppermute(mat_out, axis_name='fsdp', perm=block_next)  32.1 us
    slice x1, local copies, waits for them, and re-layouts, body(): weights[:, :, k, :]  19.2 us
    unnamed x75, local copies, waits for them, and re-layouts  18.9 us
    psum x1, waiting for transfers between devices, body(): kernel_grad = lax.psum(kernel_part, 'fsdp')  11.7 us
    reshape x1, local copies, waits for them, and re-layouts, body(): lax.all_gather(kernel, 'fsdp', axis=0, tiled=True)  10.5 us
    all_gather x1, waiting for transfers between devices, body(): lax.all_gather(kernel, 'fsdp', axis=0, tiled=True)  7.95 us
  transfers between devices with their start and end apart: 12, of which 8 were waited for; matrix products, arithmetic and copies ran while one was open for 8% of the time, Pallas kernels for 0%

profile of v1, /device:TPU:0, one launch (start us, length us, event | category | flops | bytes accessed | tf_op | source)
XLA Modules:
  0.0 363.0 jit_solution(13792615873049394136)
XLA Ops:
  8.1 2.9 collective-permute-start
  11.1 7.3 %collective-permute-done = bf16[64,2048]{1,0:T(8,128)(2,1)S(1)} collective-permute-done((bf16[64,2048]{1,0:T(8,128)(2,1)S(1)}, bf16[64,2048]{1,0:T(8,128)(2,1)S(1)}, u32[]{:S(2)}, u32[]{:S(2)}) %collective-permute-start) | collective-permute-done | bytes 262176 | tf_op jit(solution)/shard_map/ppermute | solution.py:17
  18.3 0.8 collective-permute-start.1
  19.1 12.4 %collective-permute-done.1 = bf16[64,2048]{1,0:T(8,128)(2,1)S(1)} collective-permute-done((bf16[64,2048]{1,0:T(8,128)(2,1)S(1)}, bf16[64,2048]{1,0:T(8,128)(2,1)S(1)}, u32[]{:S(2)}, u32[]{:S(2)}) %collective-permute-start.1) | collective-permute-done | bytes 262176 | tf_op jit(solution)/shard_map/ppermute | solution.py:17
  31.5 1.0 collective-permute-start.2
  32.6 12.4 %collective-permute-done.2 = bf16[64,2048]{1,0:T(8,128)(2,1)S(1)} collective-permute-done((bf16[64,2048]{1,0:T(8,128)(2,1)S(1)}, bf16[64,2048]{1,0:T(8,128)(2,1)S(1)}, u32[]{:S(2)}, u32[]{:S(2)}) %collective-permute-start.2) | collective-permute-done | bytes 262176 | tf_op jit(solution)/shard_map/ppermute | solution.py:17
  45.2 0.9 copy-done.29
  47.0 1.0 copy.192
  48.0 4.8 %all-to-all-start.1 = ((bf16[128,8,256]{0,2,1:T(8,128)(2,1)}), bf16[128,8,256]{0,2,1:T(8,128)(2,1)S(1)}, u32[]{:S(2)}, u32[]{:S(2)}) async-start(bf16[128,8,256]{0,2,1:T(8,128)(2,1)} %bitcast.30), calls=%async_computation.2 | async-start | bytes 1048576 | tf_op jit(solution)/shard_map/all_to_all | solution.py:98
  52.8 2.4 collective-permute-start.3
  55.2 1.3 collective-permute-start.4
  56.6 1.2 copy.213
  57.8 1.6 collective-permute-done.4
  59.4 2.7 fusion.53
  62.1 6.0 %all-to-all-done.1 = bf16[128,8,256]{0,2,1:T(8,128)(2,1)S(1)} async-done(((bf16[128,8,256]{0,2,1:T(8,128)(2,1)}), bf16[128,8,256]{0,2,1:T(8,128)(2,1)S(1)}, u32[]{:S(2)}, u32[]{:S(2)}) %all-to-all-start.1) | async-done | bytes 524320 | tf_op jit(solution)/shard_map/all_to_all | solution.py:98
  68.7 1.0 copy.169
  69.7 8.0 %all-gather.2.cloned.1.call-done = bf16[2048,1152]{1,0:T(8,128)(2,1)} async-done(((bf16[512,1152]{1,0:T(8,128)(2,1)}), bf16[2048,1152]{1,0:T(8,128)(2,1)}) %all-gather.2.cloned.1.call-update) | async-done | bytes 4718608 | tf_op jit(solution)/shard_map/all_gather | solution.py:69
  77.6 10.5 %reshape.88 = bf16[16,128,9,128]{3,2,1,0:T(8,128)(2,1)} reshape(bf16[2048,1152]{1,0:T(8,128)(2,1)} %all-gather.2.cloned.1.call-done) | data formatting | bytes 9437184 | tf_op jit(solution)/shard_map/reshape | solution.py:69
  88.1 19.2 %fusion.84 = (bf16[16,128,1,128]{3,2,1,0:T(2,128)(2,1)S(1)}, bf16[16,128,1,128]{3,2,1,0:T(2,128)(2,1)S(1)}, bf16[16,128,1,128]{3,2,1,0:T(2,128)(2,1)S(1)}, bf16[...) fusion(bf16[16,128,9,128]{3,2,1,0:T(8,128)(2,1)} %reshape.88), kind=kLoop, calls=%fused_computation.164 | loop fusion | bytes 9437184 | tf_op jit(solution)/shard_map/slice | solution.py:77
  107.9 0.9 copy-done.22
  109.3 0.9 copy-done.21
  115.8 0.8 fusion.14
  116.7 1.0 copy.145
  117.8 1.3 collective-permute-start.5
  119.0 1.1 copy.155
  120.1 3.8 %collective-permute-start.6 = (bf16[4,2048]{0,1:T(8,128)(2,1)}, bf16[4,2048]{0,1:T(8,128)(2,1)}, u32[]{:S(2)}, u32[]{:S(2)}) collective-permute-start(bf16[4,2048]{0,1:T(8,128)(2,1)} %copy.155), channel_id=1, source_target_pairs={{0,1},{1,2},{2,3},{3,4},{4,5},{5,6},{6,7},{8,9},{9,10},{10,11},{11... | collective-permute-start | bytes 49160 | tf_op jit(solution)/shard_map/ppermute | solution.py:35
  124.0 2.7 fusion.64
  126.7 1.0 copy.144
  127.7 4.6 %all-to-all-start = ((bf16[128,8,256]{0,2,1:T(8,128)(2,1)}), bf16[128,8,256]{0,2,1:T(8,128)(2,1)S(1)}, u32[]{:S(2)}, u32[]{:S(2)}) async-start(bf16[128,8,256]{0,2,1:T(8,128)(2,1)} %bitcast.28), calls=%async_computation.1 | async-start | bytes 1048576 | tf_op jit(solution)/shard_map/all_to_all | solution.py:99
  132.6 6.8 %pad_maximum_fusion = (bf16[128,2048]{0,1:T(8,128)(2,1)S(1)}, bf16[128,2048]{0,1:T(8,128)(2,1)S(1)}, bf16[128,2048]{0,1:T(8,128)(2,1)S(1)}, bf16[128,2048]{0,1:T...) fusion(bf16[128,2048]{0,1:T(8,128)(2,1)} %bitcast.13, ...), kind=kLoop, calls=%fused_computation.106 | loop fusion | flops 8388608 | bytes 4751360 | tf_op jit(solution)/shard_map/concatenate | solution.py:33
  139.8 0.8 copy-done.7
  141.0 0.9 copy-done.5
  142.2 0.9 copy-done.12
  143.8 0.9 copy-done.3
  145.0 0.9 copy-done.1
  146.6 0.9 copy-done.15
  147.5 1.3 convolution_add_fusion.1
  148.8 1.6 copy.191
  150.4 1.1 copy.166
  151.5 1.3 reshape.83
  152.8 1.4 fusion.10
  156.9 1.9 copy.171
  158.8 2.4 copy.284
  162.6 1.9 convolution_multiply_fusion
  164.6 39.9 %all-reduce.1 = f32[2048]{0:T(1024)S(1)} all-reduce(f32[2048]{0:T(1024)S(1)} %broadcast_multiply_fusion.1), channel_id=3, replica_groups=mesh['fsdp'=4,'seq'=8] {'fsdp','seq'}, use_global_device_ids=true, to_apply=%region_4.5.clone | all-reduce | flops 2048 | bytes 16384
  205.0 11.7 %all-reduce.4.cloned.1.call-done = f32[256,1152]{0,1:T(8,128)} async-done(((f32[256,1152]{0,1:T(8,128)}), f32[256,1152]{0,1:T(8,128)}) %all-reduce.4.cloned.1.call-update) | async-done | bytes 1179664 | tf_op jit(solution)/shard_map/psum | solution.py:132
  216.7 2.7 copy.172
  219.4 137.1 %reduce-scatter.2.cloned.1.call-done = f32[8,2048]{1,0:T(8,128)} async-done(((f32[256,2048]{1,0:T(8,128)}), f32[8,2048]{1,0:T(8,128)}) %reduce-scatter.2.cloned.1.call-update) | async-done | bytes 65552 | tf_op jit(solution)/shard_map/reduce_scatter | solution.py:147
  (110 shorter events, 16.8 us)
Async XLA Ops:
  7.2 1.0 copy-start.26
  7.2 70.5 %all-gather.2.cloned.1.call-start = ((), (), s32[]{:S(2)}) async-start(), calls=%async_computation.3 | async-start | bytes 5898240 | tf_op jit(solution)/shard_map/all_gather | solution.py:69
  8.1 10.2 %collective-permute-start = (bf16[64,2048]{1,0:T(8,128)(2,1)S(1)}, bf16[64,2048]{1,0:T(8,128)(2,1)S(1)}, u32[]{:S(2)}, u32[]{:S(2)}) collective-permute-start(bf16[64,2048]{1,0:T(8,128)(2,1)S(1)} %copy-done.26), channel_id=1, source_target_pairs={{0,8},{8,16},{16,24},{24,0},{1,9},{9,17},{17,25},{25,1},{2,10},{10... | collective-permute-start | bytes 786440 | tf_op jit(solution)/shard_map/ppermute | solution.py:17
  18.3 13.2 %collective-permute-start.1 = (bf16[64,2048]{1,0:T(8,128)(2,1)S(1)}, bf16[64,2048]{1,0:T(8,128)(2,1)S(1)}, u32[]{:S(2)}, u32[]{:S(2)}) collective-permute-start(bf16[64,2048]{1,0:T(8,128)(2,1)S(1)} %collective-permute-done), channel_id=1, source_target_pairs={{0,8},{8,16},{16,24},{24,0},{1,9},{9,17},{17,25},{25,1},{2,10},{10... | collective-permute-start | bytes 786440 | tf_op jit(solution)/shard_map/ppermute | solution.py:17
  31.5 13.4 %collective-permute-start.2 = (bf16[64,2048]{1,0:T(8,128)(2,1)S(1)}, bf16[64,2048]{1,0:T(8,128)(2,1)S(1)}, u32[]{:S(2)}, u32[]{:S(2)}) collective-permute-start(bf16[64,2048]{1,0:T(8,128)(2,1)S(1)} %collective-permute-done.1), channel_id=1, source_target_pairs={{0,8},{8,16},{16,24},{24,0},{1,9},{9,17},{17,25},{25,1},{2,10},{10... | collective-permute-start | bytes 786440 | tf_op jit(solution)/shard_map/ppermute | solution.py:17
  45.1 1.0 copy-start.29
  45.1 1.0 copy-start.31
  46.1 0.7 copy-start.30
  47.0 9.5 %copy-start.16 = (bf16[1,128,2048]{2,1,0:T(8,128)(2,1)S(1)}, bf16[1,128,2048]{2,1,0:T(8,128)(2,1)}, u32[]{:S(2)}) copy-start(bf16[1,128,2048]{2,1,0:T(8,128)(2,1)} %param.11) | copy-start | bytes 1572868
  48.0 20.1 %all-to-all-start.1 = ((bf16[128,8,256]{0,2,1:T(8,128)(2,1)}), bf16[128,8,256]{0,2,1:T(8,128)(2,1)S(1)}, u32[]{:S(2)}, u32[]{:S(2)}) async-start(bf16[128,8,256]{0,2,1:T(8,128)(2,1)} %bitcast.30), calls=%async_computation.2 | async-start | bytes 1048576 | tf_op jit(solution)/shard_map/all_to_all | solution.py:98
  52.8 5.0 %collective-permute-start.3 = (bf16[4,2048]{1,0:T(4,128)(2,1)S(1)}, bf16[4,2048]{1,0:T(4,128)(2,1)S(1)}, u32[]{:S(2)}, u32[]{:S(2)}) collective-permute-start(bf16[4,2048]{1,0:T(4,128)(2,1)S(1)} %get-tuple-element.54), channel_id=1, source_target_pairs={{0,1},{1,2},{2,3},{3,4},{4,5},{5,6},{6,7},{8,9},{9,10},{10,11},{11... | collective-permute-start | bytes 49160 | tf_op jit(solution)/shard_map/ppermute | solution.py:35
  55.2 4.2 %collective-permute-start.4 = (bf16[4,2048]{1,0:T(4,128)(2,1)S(1)}, bf16[4,2048]{1,0:T(4,128)(2,1)S(1)}, u32[]{:S(2)}, u32[]{:S(2)}) collective-permute-start(bf16[4,2048]{1,0:T(4,128)(2,1)S(1)} %get-tuple-element.53), channel_id=1, source_target_pairs={{1,0},{2,1},{3,2},{4,3},{5,4},{6,5},{7,6},{9,8},{10,9},{11,10},{12... | collective-permute-start | bytes 49160 | tf_op jit(solution)/shard_map/ppermute | solution.py:37
  88.1 19.3 %copy-start.23 = (bf16[16,16,8,128]{3,2,1,0:T(8,128)(2,1)S(1)}, bf16[16,16,8,128]{3,2,1,0:T(8,128)(2,1)}, u32[]{:S(2)}) copy-start(bf16[16,16,8,128]{3,2,1,0:T(8,128)(2,1)} %get-tuple-element.51) | copy-start | bytes 1572868
  107.3 2.0 copy-start.6
  107.3 2.0 copy-start.8
  107.3 2.0 copy-start.4
  107.3 3.4 copy-start.11
  107.3 4.6 %copy-start.10 = (bf16[16,128,1,128]{3,2,1,0:T(2,128)(2,1)}, bf16[16,128,1,128]{3,2,1,0:T(2,128)(2,1)S(1)}, u32[]{:S(2)}) copy-start(bf16[16,128,1,128]{3,2,1,0:T(2,128)(2,1)S(1)} %get-tuple-element.22) | copy-start | bytes 1572868
  107.3 5.1 %copy-start.2 = (bf16[16,128,1,128]{3,2,1,0:T(2,128)(2,1)}, bf16[16,128,1,128]{3,2,1,0:T(2,128)(2,1)S(1)}, u32[]{:S(2)}) copy-start(bf16[16,128,1,128]{3,2,1,0:T(2,128)(2,1)S(1)} %get-tuple-element.21) | copy-start | bytes 1572868
  107.3 6.1 %copy-start = (bf16[16,128,1,128]{3,2,1,0:T(2,128)(2,1)}, bf16[16,128,1,128]{3,2,1,0:T(2,128)(2,1)S(1)}, u32[]{:S(2)}) copy-start(bf16[16,128,1,128]{3,2,1,0:T(2,128)(2,1)S(1)} %get-tuple-element.20) | copy-start | bytes 1572868
  107.4 7.6 %copy-start.14 = (bf16[16,128,1,128]{3,2,1,0:T(2,128)(2,1)}, bf16[16,128,1,128]{3,2,1,0:T(2,128)(2,1)S(1)}, u32[]{:S(2)}) copy-start(bf16[16,128,1,128]{3,2,1,0:T(2,128)(2,1)S(1)} %get-tuple-element.18) | copy-start | bytes 1572868
  107.4 1.4 copy-start.22
  108.8 1.4 copy-start.21
  110.2 1.2 copy-start.20
  111.9 1.0 copy-start.19
  112.9 1.0 copy-start.18
  114.5 1.2 copy-start.25
  114.5 1.3 copy-start.27
  117.8 14.8 %collective-permute-start.5 = (bf16[4,2048]{0,1:T(8,128)(2,1)}, bf16[4,2048]{0,1:T(8,128)(2,1)}, u32[]{:S(2)}, u32[]{:S(2)}) collective-permute-start(bf16[4,2048]{0,1:T(8,128)(2,1)} %copy.145), channel_id=1, source_target_pairs={{1,0},{2,1},{3,2},{4,3},{5,4},{6,5},{7,6},{9,8},{10,9},{11,10},{12... | collective-permute-start | bytes 49160 | tf_op jit(solution)/shard_map/ppermute | solution.py:37
  120.1 12.4 %collective-permute-start.6 = (bf16[4,2048]{0,1:T(8,128)(2,1)}, bf16[4,2048]{0,1:T(8,128)(2,1)}, u32[]{:S(2)}, u32[]{:S(2)}) collective-permute-start(bf16[4,2048]{0,1:T(8,128)(2,1)} %copy.155), channel_id=1, source_target_pairs={{0,1},{1,2},{2,3},{3,4},{4,5},{5,6},{6,7},{8,9},{9,10},{10,11},{11... | collective-permute-start | bytes 49160 | tf_op jit(solution)/shard_map/ppermute | solution.py:35
  127.7 22.7 %all-to-all-start = ((bf16[128,8,256]{0,2,1:T(8,128)(2,1)}), bf16[128,8,256]{0,2,1:T(8,128)(2,1)S(1)}, u32[]{:S(2)}, u32[]{:S(2)}) async-start(bf16[128,8,256]{0,2,1:T(8,128)(2,1)} %bitcast.28), calls=%async_computation.1 | async-start | bytes 1048576 | tf_op jit(solution)/shard_map/all_to_all | solution.py:99
  132.3 84.4 %all-reduce.4.cloned.1.call-start = ((), (), s32[]{:S(2)}) async-start(), calls=%async_computation.5 | async-start | bytes 2359296 | tf_op jit(solution)/shard_map/psum | solution.py:132
  132.6 6.9 %copy-start.9 = (bf16[16,128,1,128]{3,2,1,0:T(2,128)(2,1)S(1)}, bf16[16,128,1,128]{3,2,1,0:T(2,128)(2,1)}, u32[]{:S(2)}) copy-start(bf16[16,128,1,128]{3,2,1,0:T(2,128)(2,1)} %copy-done.8) | copy-start | bytes 1572868
  139.4 1.2 copy-start.7
  140.7 1.2 copy-start.5
  141.9 1.2 copy-start.12
  141.9 1.5 copy-start.13
  143.4 1.2 copy-start.3
  144.6 1.2 copy-start.1
  146.2 1.2 copy-start.15
  152.8 1.4 copy-start.28
  161.2 1.0 copy-start.17
  161.2 195.3 %reduce-scatter.2.cloned.1.call-start = ((), (), s32[]{:S(2)}) async-start(), calls=%async_computation.4 | async-start | bytes 2162688 | tf_op jit(solution)/shard_map/reduce_scatter | solution.py:147
  162.6 1.9 copy-start.24
Sparse Core Ops, SparseCore 0:
  9.8 67.7 all-gather.1
  161.3 55.4 all-reduce.3
  219.7 136.7 reduce-scatter.1
